TPU v7x, 128 devices: a whole 4x4x4 slice. The times are simulated.
128 devices in a mesh: cell: 32 (over y, z, core), own: 4 (over x).
Axes of the slice: x: 4, y: 4, z: 4, core: 2. Of those that a mesh axis runs over, the one named last changes fastest.
Arguments:
- hist: bfloat16 [262144, 3, 256], P(('cell', 'own')), as said below
- dest: int32 [262144, 1], P(('cell', 'own')), may hold values from 0 to 127; in each aligned block of 2048 rows (0 to 2047, 2048 to 4095, ...) at most 32 rows name the same one
- cell_in: int32 [262144], P(('cell', 'own')), may hold values from 0 to 1023
- offsets: int32 [4, 131072], P(None, ('cell', 'own')), may hold values from -4 to 4
Outputs:
- multipliers: float32 [2, 6, 131072], P(None, None, ('cell', 'own'))
- fit_stat: float32 [2, 131072], P(None, ('cell', 'own'))
Inputs may be any that keep to these rules, and one draw needn't show every extreme that they name: `dest`: the rows of one device name each cell block at most 32 times, and in every draw some device names some block exactly 32 times. `hist`: Positive, every entry at least three ten-thousandths of its row's largest.
All inputs are finite; a program needn't handle non-finite values.
Results may differ from a plain program's by a relative error of at most 0.0022.
Values may be sent and summed in bfloat16 or wider, within the bound.
No kernel may reach another device: no remote copies, remote signals or barrier semaphores. Data moves between devices by JAX's collectives and lax.ppermute only.
A program may use at most 64 MiB of HBM per device.

v0:
```python
import jax
import jax.numpy as jnp
import numpy as np
from jax import lax
from jax.experimental import pallas as pl
from jax.experimental.pallas import tpu as pltpu
from jax.sharding import PartitionSpec as P

SPEC = 2
MOM = 6
NEWTON = 8
W = 4
CODE = 32
EXTRA = 8
LOOP_PRECISION = lax.Precision.HIGH


def pair_list(count):
    return [(row, col) for row in range(count) for col in range(row + 1)]


def chol_solve(hess, rhs, count):
    lower = [[None] * count for _ in range(count)]
    for row in range(count):
        for col in range(row + 1):
            total = hess[row][col]
            for inner in range(col):
                total = total - lower[row][inner] * lower[col][inner]
            if row == col:
                lower[row][col] = jnp.sqrt(total)
            else:
                lower[row][col] = total / lower[col][col]
    forward = []
    for row in range(count):
        total = rhs[row]
        for inner in range(row):
            total = total - lower[row][inner] * forward[inner]
        forward.append(total / lower[row][row])
    backward = [None] * count
    for row in reversed(range(count)):
        total = forward[row]
        for inner in range(row + 1, count):
            total = total - lower[inner][row] * backward[inner]
        backward[row] = total / lower[row][row]
    return backward


def newton_step(got, moments, lam, count):
    pairs = pair_list(count)
    norm = got[count]
    first = [got[m] / norm for m in range(count)]
    hess = [[None] * count for _ in range(count)]
    for k, (row, col) in enumerate(pairs):
        second = got[count + 1 + k] / norm
        value = second - first[row] * first[col]
        if row == col:
            value = value + 0.01
        hess[row][col] = value
    rhs = [first[m] - moments[m] for m in range(count)]
    delta = chol_solve(hess, rhs, count)
    return [lam[m] - 0.5 * delta[m] for m in range(count)]


def fit_kernel(
    h_ref, rim_ref, w_ref, phit_ref, psi_ref, lam_ref, fit_ref, lam_s, dense_ref, t_ref, ext_ref
):
    spec, levels, cells = h_ref.shape
    pad = (ext_ref.shape[2] - cells) // 2
    rim = rim_ref.shape[2] // 2
    ext_ref[...] = jnp.zeros(ext_ref.shape, jnp.float32)
    for s in range(spec):
        field = h_ref[s]
        t_ref[s] = field
        lower = jnp.concatenate([jnp.zeros((1, cells), jnp.float32), t_ref[s, : levels - 1, :]], axis=0)
        upper = jnp.concatenate([t_ref[s, 1:, :], jnp.zeros((1, cells), jnp.float32)], axis=0)
        levelled = 0.5 * field + 0.25 * (lower + upper)
        ext_ref[s, :, pad : pad + cells] = levelled
        ext_ref[s, :, pad - rim : pad] = rim_ref[s, :, :rim]
        ext_ref[s, :, pad + cells : pad + cells + rim] = rim_ref[s, :, rim:]
        target = 1.0 + levelled
        for k in range(w_ref.shape[0]):
            shift = k - w_ref.shape[0] // 2
            target = target + w_ref[k : k + 1, :] * ext_ref[s, :, pad + shift : pad + shift + cells]
        t_ref[s] = target
    count = lam_ref.shape[0]
    used = count + 1 + len(pair_list(count))
    groups = 8 // spec
    part = cells // groups
    highest = lax.Precision.HIGHEST

    def contract(a, b, precision=highest):
        return jnp.dot(a, b, precision=precision, preferred_element_type=jnp.float32)

    def densify(gots):
        for s in range(spec):
            for j in range(groups):
                piece = gots[s][:, j * part : (j + 1) * part]
                row = s * groups + j
                for k in range(used):
                    dense_ref[k, row : row + 1, :] = piece[k : k + 1, :]
        return [dense_ref[k] for k in range(used)]

    def spread(values):
        for m in range(count):
            for s in range(spec):
                for j in range(groups):
                    row = s * groups + j
                    lam_s[s, m : m + 1, j * part : (j + 1) * part] = values[m][row : row + 1, :]

    got = densify([contract(psi_ref[...], t_ref[s], LOOP_PRECISION) for s in range(spec)])
    moments = [got[m] / got[count] for m in range(count)]
    lam_s[...] = jnp.zeros(lam_s.shape, jnp.float32)
    zero = jnp.zeros((8, part), jnp.float32)

    def step(_, lam):
        gots = []
        for s in range(spec):
            expo = jnp.exp(contract(phit_ref[...], lam_s[s], LOOP_PRECISION))
            gots.append(contract(psi_ref[...], expo, LOOP_PRECISION))
        new = newton_step(densify(gots), moments, list(lam), count)
        spread(new)
        return tuple(new)

    lax.fori_loop(0, NEWTON, step, tuple([zero] * count))
    for s in range(spec):
        target = t_ref[s]
        exponent = contract(phit_ref[...], lam_s[s])
        log_norm = jnp.log(jnp.sum(jnp.exp(exponent), axis=0, keepdims=True))
        whole = jnp.sum(target, axis=0, keepdims=True)
        ratio = jnp.log(target / whole) - (exponent - log_norm)
        fit_ref[s : s + 1, :] = 2.0 * jnp.sum(target * ratio, axis=0, keepdims=True) / levels
        for m in range(count):
            lam_ref[m, s : s + 1, :] = lam_s[s, m : m + 1, :]


def legendre_numpy(levels, count):
    xpos = (2.0 * np.arange(levels, dtype=np.float64) + 1.0) / levels - 1.0
    prev = np.ones_like(xpos)
    curr = xpos
    table = [curr]
    for order in range(1, count):
        nxt = ((2 * order + 1) * xpos * curr - order * prev) / (order + 1)
        prev, curr = (curr, nxt)
        table.append(curr)
    return np.stack(table, axis=0).astype(np.float32)


def fit_all(cellhist, rim, weights, count):
    spec, levels, cells = cellhist.shape
    phi = legendre_numpy(levels, count)
    pairs = pair_list(count)
    width = 8
    phit = np.zeros((levels, width), np.float32)
    phit[:, :count] = phi.T
    rows = [phi[m] for m in range(count)] + [np.ones((levels,), np.float32)]
    rows += [phi[r] * phi[c] for r, c in pairs]
    height = -(-len(rows) // 8) * 8
    rows += [np.zeros((levels,), np.float32)] * (height - len(rows))
    psi = np.stack(rows, axis=0)
    lam, fit = pl.pallas_call(
        fit_kernel,
        out_shape=(
            jax.ShapeDtypeStruct((count, spec, cells), jnp.float32),
            jax.ShapeDtypeStruct((spec, cells), jnp.float32),
        ),
        scratch_shapes=[
            pltpu.VMEM((spec, width, cells), jnp.float32),
            pltpu.VMEM((height, 8, cells * spec // 8), jnp.float32),
            pltpu.VMEM((spec, levels, cells), jnp.float32),
            pltpu.VMEM((spec, levels, cells + 256), jnp.float32),
        ],
    )(cellhist, rim, weights, jnp.asarray(phit), jnp.asarray(psi))
    return jnp.transpose(lam, (1, 0, 2)), fit


def smooth_levels(field):
    padded = jnp.pad(field, ((0, 0), (1, 1), (0, 0)))
    return 0.5 * field + 0.25 * (padded[:, :-2, :] + padded[:, 2:, :])


def body_inner(hist, dest, cell_in, offsets):
    rows = hist.shape[0]
    width = hist.shape[2]
    cells = offsets.shape[1]
    devices = lax.axis_size(("cell", "own"))
    capacity = 2 * rows // devices
    slots = devices * capacity
    packed = jnp.sum(hist, axis=1, dtype=jnp.float32).astype(jnp.bfloat16)
    target_block = dest[:, 0]
    member = (target_block[:, None] == jnp.arange(devices, dtype=jnp.int32)[None, :]).astype(
        jnp.int32
    )
    ranks = jnp.sum((jnp.cumsum(member, axis=0) - 1) * member, axis=1)
    position = target_block * capacity + ranks
    codes = jnp.stack([cell_in // CODE + 1, cell_in % CODE], axis=1).astype(jnp.bfloat16)
    codes = jnp.pad(codes, ((0, 0), (0, 128 - 2)))
    payload = jnp.concatenate([packed, codes], axis=1)
    place = (jnp.arange(slots, dtype=jnp.int32)[:, None] == position[None, :]).astype(jnp.bfloat16)
    sent = jnp.dot(place, payload, preferred_element_type=jnp.float32)
    narrow = width // SPEC
    halves = [
        sent[:, h * narrow : (h + 1) * narrow].astype(jnp.bfloat16).reshape(devices, capacity, narrow)
        for h in range(SPEC)
    ]
    code_rows = sent[:, width : width + 2].reshape(devices, capacity, 2)
    code_rows = jnp.swapaxes(code_rows, 1, 2).astype(jnp.bfloat16)
    code_rows = jnp.pad(code_rows, ((0, 0), (0, EXTRA - 2), (0, narrow - capacity)))
    message = jnp.concatenate(halves + [code_rows], axis=1)
    got = lax.all_to_all(message, ("cell", "own"), split_axis=0, concat_axis=0, tiled=True)
    recv_halves = [
        got[:, h * capacity : (h + 1) * capacity, :].reshape(slots, narrow) for h in range(SPEC)
    ]
    high = got[:, SPEC * capacity, :capacity].astype(jnp.int32).reshape(slots)
    low = got[:, SPEC * capacity + 1, :capacity].astype(jnp.int32).reshape(slots)
    recv_cells = jnp.where(high > 0, (high - 1) * CODE + low, -1)

    def cell_sums(picked):
        return jnp.stack(
            [
                lax.dot_general(
                    part, picked, (((0,), (0,)), ((), ())), preferred_element_type=jnp.float32
                )
                for part in recv_halves
            ]
        )

    edges = jnp.concatenate(
        [jnp.arange(W, dtype=jnp.int32), jnp.arange(cells - W, cells, dtype=jnp.int32)]
    )
    edge_lev = smooth_levels(cell_sums((recv_cells[:, None] == edges[None, :]).astype(jnp.bfloat16)))
    forward = [(i, i + 1) for i in range(devices - 1)]
    backward = [(target, source) for source, target in forward]
    below = lax.ppermute(edge_lev[:, :, W:], ("cell", "own"), forward)
    above = lax.ppermute(edge_lev[:, :, :W], ("cell", "own"), backward)
    select = (recv_cells[:, None] == jnp.arange(cells, dtype=jnp.int32)[None, :]).astype(
        jnp.bfloat16
    )
    cellhist = cell_sums(select)
    weights = jnp.stack(
        [jnp.sum((offsets == shift).astype(jnp.float32), axis=0) for shift in range(-W, W + 1)]
    )
    rim = jnp.concatenate([below, above], axis=2)
    return fit_all(cellhist, rim, weights, MOM)


def solution(mesh):
    placed = (
        P(("cell", "own"), None, None),
        P(("cell", "own"), None),
        P(("cell", "own")),
        P(None, ("cell", "own")),
    )
    return jax.shard_map(
        body_inner,
        mesh=mesh,
        in_specs=placed,
        out_specs=(P(None, None, ("cell", "own")), P(None, ("cell", "own"))),
        check_vma=False,
    )
```

profile of v0, /device:TPU:8, one launch (start us, length us, event | category | flops | bytes accessed | tf_op | source)
XLA Modules:
  0.0 98.0 jit_solution(7443576494747832241)
XLA Ops:
  0.6 0.9 copy.31
  1.5 0.3 fusion.18
  1.9 0.1 add_add_fusion
  2.0 0.0 copy-start
  2.0 0.3 copy.32
  2.4 0.6 fusion.17
  3.1 1.1 %copy.36 = bf16[2048,2]{1,0:T(8,128)(2,1)} copy(bf16[2048,2]{0,1:T(2,128)(2,1)S(1)} %pad_maximum_fusion.1) | data formatting | bytes 16384
  4.2 1.7 %reduce_sum.103 = bf16[2048,256]{1,0:T(8,128)(2,1)} reduce(bf16[2048,3,256]{2,0,1:T(8,128)(2,1)S(1)} %copy-done, bf16[]{:T(256)} %constant.32.clone.1), dimensions={1}, to_apply=%region_3.4 | reduce | flops 1048576 | bytes 4194306 | tf_op jit(solution)/shard_map/reduce_sum | solution.py:188
  5.9 10.4 %fusion.6 = bf16[4096,384]{1,0:T(8,128)(2,1)S(1)} fusion(s32[2048]{0:T(1024)S(1)} %multiply_add_fusion, bf16[2048,2]{1,0:T(8,128)(2,1)} %copy.36, bf16[2048,256]{1,0:T(8,128)(2,1)} %reduce_sum.103), kind=kOutput, calls=%fused_computation.8 | convolution fusion | flops 6457131008 | bytes 4210688 | tf_op jit(solution)/shard_map/dot_general | solution.py:199
  16.4 0.1 slice.59
  16.4 0.1 fusion.41
  16.6 0.8 copy.34
  17.4 1.7 %fusion.9 = bf16[128,72,128]{2,1,0:T(8,128)(2,1)} fusion(bf16[128,2,32]{2,1,0:T(2,128)(2,1)S(1)} %bitcast.45, bf16[128,32,128]{2,1,0:T(8,128)(2,1)S(1)} %bitcast.39, bf16[128,32,128]{2,1,0:T(8,128)(2,1)S(1)} %bitcast.38), kind=kLoop, calls=%fused_computation.13 | loop fusion | flops 9437184 | bytes 4472832 | tf_op jit(solution)/shard_map/concatenate | solution.py:208
  19.1 10.5 %all-to-all-start = ((bf16[128,72,128]{2,1,0:T(8,128)(2,1)}), bf16[128,72,128]{2,1,0:T(8,128)(2,1)S(1)}, u32[]{:S(2)}, u32[]{:S(2)}) async-start(bf16[128,72,128]{2,1,0:T(8,128)(2,1)} %fusion.9), calls=%async_computation | async-start | bytes 4718592 | tf_op jit(solution)/shard_map/all_to_all | solution.py:209
  29.6 0.1 convert_reduce_fusion
  29.7 1.3 %stack.78.w_ref = f32[9,1024]{1,0:T(8,128)} concatenate(f32[1,1024]{1,0:T(1,128)S(1)} %bitcast.56, f32[1,1024]{1,0:T(1,128)S(1)} %bitcast.55, f32[1,1024]{1,0:T(1,128)S(1)} %bitcast.54, f32[1,1024]{1,0:T(1,128)S(1)} %bitcast.53, f32[1,1024]{1,0:T(1,128)S(1)} %bitcast.52, f32[1,1024]{1,0:T(1,128)S(1)} %bitcast.51, f32[1,1024]{1,0:T(1,128)S(1)} %bitcast.50, ...), dimensions={0} | concatenate | bytes 73728 | tf_op jit(solution)/shard_map/stack | solution.py:239
  30.9 0.1 pad_add_fusion
  31.0 31.0 %all-to-all-done = bf16[128,72,128]{2,1,0:T(8,128)(2,1)S(1)} async-done(((bf16[128,72,128]{2,1,0:T(8,128)(2,1)}), bf16[128,72,128]{2,1,0:T(8,128)(2,1)S(1)}, u32[]{:S(2)}, u32[]{:S(2)}) %all-to-all-start) | async-done | bytes 2359328 | tf_op jit(solution)/shard_map/all_to_all | solution.py:209
  62.0 0.4 fusion.24
  62.4 0.1 reshape.79
  62.5 0.4 fusion.42
  62.9 3.3 %fusion.16 = f32[1,128,1024]{2,1,0:T(8,128)S(1)} fusion(bf16[4096,128]{1,0:T(8,128)(2,1)S(1)} %bitcast.43, s32[4096]{0:T(1024)S(1)} %reshape.79), kind=kOutput, calls=%fused_computation.19 | convolution fusion | flops 1077936128 | bytes 1589248 | tf_op jit(solution)/shard_map/dot_general | solution.py:220
  66.1 3.3 %fusion.15 = f32[1,128,1024]{2,1,0:T(8,128)S(1)} fusion(bf16[4096,128]{1,0:T(8,128)(2,1)S(1)} %bitcast.41, s32[4096]{0:T(1024)S(1)} %reshape.79), kind=kOutput, calls=%fused_computation.18 | convolution fusion | flops 1077936128 | bytes 1589248 | tf_op jit(solution)/shard_map/dot_general | solution.py:220
  69.4 0.3 convolution_bitcast_fusion
  69.7 0.3 convolution_bitcast_fusion.1
  70.0 0.1 fusion.35
  70.1 3.4 %collective-permute-start.1 = (f32[2,128,4]{1,2,0:T(4,128)S(1)}, f32[2,128,4]{1,2,0:T(4,128)S(1)}, u32[]{:S(2)}, u32[]{:S(2)}) collective-permute-start(f32[2,128,4]{1,2,0:T(4,128)S(1)} %get-tuple-element.20), channel_id=1, source_target_pairs={{1,0},{2,1},{3,2},{4,3},{5,4},{6,5},{7,6},{8,7},{9,8},{10,9},{11,1... | collective-permute-start | bytes 12296 | tf_op jit(solution)/shard_map/ppermute | solution.py:234
  73.5 2.5 %collective-permute-start = (f32[2,128,4]{1,2,0:T(4,128)S(1)}, f32[2,128,4]{1,2,0:T(4,128)S(1)}, u32[]{:S(2)}, u32[]{:S(2)}) collective-permute-start(f32[2,128,4]{1,2,0:T(4,128)S(1)} %get-tuple-element.19), channel_id=1, source_target_pairs={{0,1},{1,2},{2,3},{3,4},{4,5},{5,6},{6,7},{7,8},{8,9},{9,10},{10,1... | collective-permute-start | bytes 12296 | tf_op jit(solution)/shard_map/ppermute | solution.py:233
  76.0 1.1 %pad_maximum_fusion.h_ref = f32[2,128,1024]{2,1,0:T(8,128)} fusion(f32[1,128,1024]{2,1,0:T(8,128)S(1)} %fusion.16, f32[1,128,1024]{2,1,0:T(8,128)S(1)} %fusion.15), kind=kLoop, calls=%fused_computation.22 | loop fusion | flops 262144 | bytes 2097152 | tf_op jit(solution)/shard_map/stack | solution.py:218
  77.1 5.6 %collective-permute-done = f32[2,128,4]{1,2,0:T(4,128)S(1)} collective-permute-done((f32[2,128,4]{1,2,0:T(4,128)S(1)}, f32[2,128,4]{1,2,0:T(4,128)S(1)}, u32[]{:S(2)}, u32[]{:S(2)}) %collective-permute-start) | collective-permute-done | bytes 4128 | tf_op jit(solution)/shard_map/ppermute | solution.py:233
  82.7 0.8 copy.35.rim_ref
  83.4 14.5 %shard_map.77 = (f32[6,2,1024]{2,1,0:T(2,128)}, f32[2,1024]{1,0:T(2,128)}) custom-call(f32[2,128,1024]{2,1,0:T(8,128)} %pad_maximum_fusion.h_ref, f32[2,128,8]{2,1,0:T(8,128)} %copy.35.rim_ref, f32[9,1024]{1,0:T(8,128)} %stack.78.w_ref, f32[128,8]{1,0:T(8,128)} %constant.73.clone.phit_ref, f32[32,128]{1,0:T(8,128)} %constant.74.clone.psi_ref), custom_call_target="tpu_custom_call" | custom-call | tf_op jit(solution)/shard_map/pallas_call | solution.py:160
  (21 shorter events, 0.1 us)
Async XLA Ops:
  0.6 1.7 %copy-start.1 = (s32[2048,1]{0,1:T(1,128)S(1)}, s32[2048,1]{0,1:T(1,128)}, u32[]{:S(2)}) copy-start(s32[2048,1]{0,1:T(1,128)} %param.7) | copy-start | bytes 24580
  1.5 1.5 %copy-start.3 = (s32[2048]{0:T(1024)S(1)}, s32[2048]{0:T(1024)}, u32[]{:S(2)}) copy-start(s32[2048]{0:T(1024)} %param.8) | copy-start | bytes 24580
  2.0 2.2 %copy-start = (bf16[2048,3,256]{2,0,1:T(8,128)(2,1)S(1)}, bf16[2048,3,256]{2,0,1:T(8,128)(2,1)}, u32[]{:S(2)}) copy-start(bf16[2048,3,256]{2,0,1:T(8,128)(2,1)} %param.6) | copy-start | bytes 9437188
  19.1 10.5 %copy-start.2 = (s32[4,1024]{1,0:T(4,128)S(1)}, s32[4,1024]{1,0:T(4,128)}, u32[]{:S(2)}) copy-start(s32[4,1024]{1,0:T(4,128)} %param.9) | copy-start | bytes 49156
  19.1 43.0 %all-to-all-start = ((bf16[128,72,128]{2,1,0:T(8,128)(2,1)}), bf16[128,72,128]{2,1,0:T(8,128)(2,1)S(1)}, u32[]{:S(2)}, u32[]{:S(2)}) async-start(bf16[128,72,128]{2,1,0:T(8,128)(2,1)} %fusion.9), calls=%async_computation | async-start | bytes 4718592 | tf_op jit(solution)/shard_map/all_to_all | solution.py:209
  70.1 7.0 %collective-permute-start.1 = (f32[2,128,4]{1,2,0:T(4,128)S(1)}, f32[2,128,4]{1,2,0:T(4,128)S(1)}, u32[]{:S(2)}, u32[]{:S(2)}) collective-permute-start(f32[2,128,4]{1,2,0:T(4,128)S(1)} %get-tuple-element.20), channel_id=1, source_target_pairs={{1,0},{2,1},{3,2},{4,3},{5,4},{6,5},{7,6},{8,7},{9,8},{10,9},{11,1... | collective-permute-start | bytes 12296 | tf_op jit(solution)/shard_map/ppermute | solution.py:234
  73.5 9.1 %collective-permute-start = (f32[2,128,4]{1,2,0:T(4,128)S(1)}, f32[2,128,4]{1,2,0:T(4,128)S(1)}, u32[]{:S(2)}, u32[]{:S(2)}) collective-permute-start(f32[2,128,4]{1,2,0:T(4,128)S(1)} %get-tuple-element.19), channel_id=1, source_target_pairs={{0,1},{1,2},{2,3},{3,4},{4,5},{5,6},{6,7},{7,8},{8,9},{9,10},{10,1... | collective-permute-start | bytes 12296 | tf_op jit(solution)/shard_map/ppermute | solution.py:233
where the time goes:
time: 98.3 us; the launch traced here: 98 us
  waiting for transfers between devices  36.6 us (37%)
  matrix products  17.5 us (18%)
  starting transfers between devices  16.3 us (17%)
  Pallas kernels  14.5 us (15%)
  other arithmetic  6.3 us (6%)
  local copies, waits for them, and re-layouts  5.85 us (6%)
    all_to_all x1, waiting for transfers between devices, body_inner(): lax.all_to_all(message, ('cell', 'own'), split_axis=0, concat_axis=0, til...  31 us
    pallas_call x1, Pallas kernels, fit_all(): pl.pallas_call(fit_kernel, out_shape=(jax.ShapeDtypeStruct((count, spec,...  14.5 us
    all_to_all x1, starting transfers between devices, body_inner(): lax.all_to_all(message, ('cell', 'own'), split_axis=0, concat_axis=0, til...  10.5 us
    dot_general x1, matrix products, body_inner(): sent = jnp.dot(place, payload, preferred_element_type=jnp.float32)  10.4 us
    dot_general x4, matrix products, cell_sums(): lax.dot_general(part, picked, (((0,), (0,)), ((), ())), preferred_element...  7.13 us
    ppermute x1, waiting for transfers between devices, body_inner(): below = lax.ppermute(edge_lev[:, :, W:], ('cell', 'own'), forward)  5.56 us
    ppermute x1, starting transfers between devices, body_inner(): above = lax.ppermute(edge_lev[:, :, :W], ('cell', 'own'), backward)  3.39 us
    ppermute x1, starting transfers between devices, body_inner(): below = lax.ppermute(edge_lev[:, :, W:], ('cell', 'own'), forward)  2.46 us
  transfers between devices with their start and end apart: 3, of which 2 were waited for; matrix products, arithmetic and copies ran while one was open for 3% of the time, Pallas kernels for 0%

commit v1 on v0

--- a/solution.py
+++ b/solution.py
@@ -107,7 +107,7 @@
                     row = s * groups + j
                     lam_s[s, m : m + 1, j * part : (j + 1) * part] = values[m][row : row + 1, :]
 
-    got = densify([contract(psi_ref[...], t_ref[s], LOOP_PRECISION) for s in range(spec)])
+    got = densify([contract(psi_ref[...], t_ref[s]) for s in range(spec)])
     moments = [got[m] / got[count] for m in range(count)]
     lam_s[...] = jnp.zeros(lam_s.shape, jnp.float32)
     zero = jnp.zeros((8, part), jnp.float32)
@@ -192,8 +192,10 @@
     )
     ranks = jnp.sum((jnp.cumsum(member, axis=0) - 1) * member, axis=1)
     position = target_block * capacity + ranks
-    codes = jnp.stack([cell_in // CODE + 1, cell_in % CODE], axis=1).astype(jnp.bfloat16)
-    codes = jnp.pad(codes, ((0, 0), (0, 128 - 2)))
+    column = jnp.arange(128, dtype=jnp.int32)[None, :]
+    codes = jnp.where(
+        column == 0, cell_in[:, None] // CODE + 1, jnp.where(column == 1, cell_in[:, None] % CODE, 0)
+    ).astype(jnp.bfloat16)
     payload = jnp.concatenate([packed, codes], axis=1)
     place = (jnp.arange(slots, dtype=jnp.int32)[:, None] == position[None, :]).astype(jnp.bfloat16)
     sent = jnp.dot(place, payload, preferred_element_type=jnp.float32)

time: 98.3 us -> 99.4 us (1.011)
  other arithmetic: 6.3 us -> 7.57 us
    convert_element_type x0 -> x1, other arithmetic: none -> 1.29 us  [body_inner(): codes = jnp.where(column == 0, cell_in[:, None] // CODE + 1, jnp.where(co...]
where the time goes in v1:
time: 99.4 us; the launch traced here: 99 us
  waiting for transfers between devices  36.6 us (37%)
  matrix products  17.4 us (18%)
  starting transfers between devices  16.3 us (16%)
  Pallas kernels  14.7 us (15%)
  other arithmetic  7.57 us (8%)
  local copies, waits for them, and re-layouts  5.59 us (6%)
    all_to_all x1, waiting for transfers between devices, body_inner(): lax.all_to_all(message, ('cell', 'own'), split_axis=0, concat_axis=0, til...  31 us
    pallas_call x1, Pallas kernels, fit_all(): pl.pallas_call(fit_kernel, out_shape=(jax.ShapeDtypeStruct((count, spec,...  14.7 us
    all_to_all x1, starting transfers between devices, body_inner(): lax.all_to_all(message, ('cell', 'own'), split_axis=0, concat_axis=0, til...  10.4 us
    dot_general x1, matrix products, body_inner(): sent = jnp.dot(place, payload, preferred_element_type=jnp.float32)  10.3 us
    dot_general x4, matrix products, cell_sums(): lax.dot_general(part, picked, (((0,), (0,)), ((), ())), preferred_element...  7.12 us
    ppermute x1, waiting for transfers between devices, body_inner(): below = lax.ppermute(edge_lev[:, :, W:], ('cell', 'own'), forward)  5.56 us
    ppermute x1, starting transfers between devices, body_inner(): above = lax.ppermute(edge_lev[:, :, :W], ('cell', 'own'), backward)  3.39 us
    ppermute x1, starting transfers between devices, body_inner(): below = lax.ppermute(edge_lev[:, :, W:], ('cell', 'own'), forward)  2.46 us
  transfers between devices with their start and end apart: 3, of which 2 were waited for; matrix products, arithmetic and copies ran while one was open for 3% of the time, Pallas kernels for 0%

profile of v1, /device:TPU:8, one launch (start us, length us, event | category | flops | bytes accessed | tf_op | source)
XLA Modules:
  0.0 99.0 jit_solution(1763285765448270374)
XLA Ops:
  0.7 0.8 copy.28
  1.5 0.3 fusion.15
  1.9 0.1 add_add_fusion
  2.0 0.3 copy.29
  2.4 0.6 fusion.14
  3.0 0.8 copy-done
  3.9 1.7 %reduce_sum.103 = bf16[2048,256]{1,0:T(8,128)(2,1)} reduce(bf16[2048,3,256]{2,0,1:T(8,128)(2,1)S(1)} %copy-done, bf16[]{:T(256)} %constant.32.clone.1), dimensions={1}, to_apply=%region_3.4 | reduce | flops 1048576 | bytes 4194306 | tf_op jit(solution)/shard_map/reduce_sum | solution.py:188
  5.6 1.3 %select_convert_fusion = bf16[2048,128]{1,0:T(8,128)(2,1)S(1)} fusion(s32[2048]{0:T(1024)S(1)} %get-tuple-element.22, s32[2048]{0:T(1024)S(1)} %get-tuple-element.21, pred[128]{0:T(512)(128)(4,1)S(1)} %get-tuple-element.23, pred[128]{0:T(512)(128)(4,1)S(1)} %get-tuple-element.24), kind=kLoop, calls=%fused_computation.22 | loop fusion | flops 786432 | bytes 540928 | tf_op jit(solution)/shard_map/convert_element_type | solution.py:198
  6.9 10.3 %fusion.6 = bf16[4096,384]{1,0:T(8,128)(2,1)S(1)} fusion(s32[2048]{0:T(1024)S(1)} %multiply_add_fusion, bf16[2048,128]{1,0:T(8,128)(2,1)S(1)} %select_convert_fusion, bf16[2048,256]{1,0:T(8,128)(2,1)} %reduce_sum.103), kind=kOutput, calls=%fused_computation.8 | convolution fusion | flops 6455558144 | bytes 4726784 | tf_op jit(solution)/shard_map/dot_general | solution.py:201
  17.2 0.1 slice.59
  17.3 0.1 fusion.33
  17.5 0.8 copy.30
  18.3 1.7 %fusion.8 = bf16[128,72,128]{2,1,0:T(8,128)(2,1)} fusion(bf16[128,2,32]{2,1,0:T(2,128)(2,1)S(1)} %bitcast.45, bf16[128,32,128]{2,1,0:T(8,128)(2,1)S(1)} %bitcast.39, bf16[128,32,128]{2,1,0:T(8,128)(2,1)S(1)} %bitcast.38), kind=kLoop, calls=%fused_computation.11 | loop fusion | flops 9437184 | bytes 4472832 | tf_op jit(solution)/shard_map/concatenate | solution.py:210
  20.0 10.4 %all-to-all-start = ((bf16[128,72,128]{2,1,0:T(8,128)(2,1)}), bf16[128,72,128]{2,1,0:T(8,128)(2,1)S(1)}, u32[]{:S(2)}, u32[]{:S(2)}) async-start(bf16[128,72,128]{2,1,0:T(8,128)(2,1)} %fusion.8), calls=%async_computation | async-start | bytes 4718592 | tf_op jit(solution)/shard_map/all_to_all | solution.py:211
  30.4 0.1 convert_reduce_fusion
  30.5 1.3 %stack.63.w_ref = f32[9,1024]{1,0:T(8,128)} concatenate(f32[1,1024]{1,0:T(1,128)S(1)} %bitcast.56, f32[1,1024]{1,0:T(1,128)S(1)} %bitcast.55, f32[1,1024]{1,0:T(1,128)S(1)} %bitcast.54, f32[1,1024]{1,0:T(1,128)S(1)} %bitcast.53, f32[1,1024]{1,0:T(1,128)S(1)} %bitcast.52, f32[1,1024]{1,0:T(1,128)S(1)} %bitcast.51, f32[1,1024]{1,0:T(1,128)S(1)} %bitcast.50, ...), dimensions={0} | concatenate | bytes 73728 | tf_op jit(solution)/shard_map/stack | solution.py:241
  31.8 0.1 pad_add_fusion
  31.9 31.0 %all-to-all-done = bf16[128,72,128]{2,1,0:T(8,128)(2,1)S(1)} async-done(((bf16[128,72,128]{2,1,0:T(8,128)(2,1)}), bf16[128,72,128]{2,1,0:T(8,128)(2,1)S(1)}, u32[]{:S(2)}, u32[]{:S(2)}) %all-to-all-start) | async-done | bytes 2359328 | tf_op jit(solution)/shard_map/all_to_all | solution.py:211
  62.9 0.4 fusion.20
  63.3 0.1 reshape.116
  63.4 0.4 fusion.34
  63.7 3.3 %fusion.13 = f32[1,128,1024]{2,1,0:T(8,128)S(1)} fusion(bf16[4096,128]{1,0:T(8,128)(2,1)S(1)} %bitcast.43, s32[4096]{0:T(1024)S(1)} %reshape.116), kind=kOutput, calls=%fused_computation.16 | convolution fusion | flops 1077936128 | bytes 1589248 | tf_op jit(solution)/shard_map/dot_general | solution.py:222
  67.0 3.3 %fusion.12 = f32[1,128,1024]{2,1,0:T(8,128)S(1)} fusion(bf16[4096,128]{1,0:T(8,128)(2,1)S(1)} %bitcast.41, s32[4096]{0:T(1024)S(1)} %reshape.116), kind=kOutput, calls=%fused_computation.15 | convolution fusion | flops 1077936128 | bytes 1589248 | tf_op jit(solution)/shard_map/dot_general | solution.py:222
  70.3 0.3 convolution_bitcast_fusion
  70.6 0.3 convolution_bitcast_fusion.1
  70.9 0.1 fusion.29
  71.0 3.4 %collective-permute-start.1 = (f32[2,128,4]{1,2,0:T(4,128)S(1)}, f32[2,128,4]{1,2,0:T(4,128)S(1)}, u32[]{:S(2)}, u32[]{:S(2)}) collective-permute-start(f32[2,128,4]{1,2,0:T(4,128)S(1)} %get-tuple-element.20), channel_id=1, source_target_pairs={{1,0},{2,1},{3,2},{4,3},{5,4},{6,5},{7,6},{8,7},{9,8},{10,9},{11,1... | collective-permute-start | bytes 12296 | tf_op jit(solution)/shard_map/ppermute | solution.py:236
  74.4 2.5 %collective-permute-start = (f32[2,128,4]{1,2,0:T(4,128)S(1)}, f32[2,128,4]{1,2,0:T(4,128)S(1)}, u32[]{:S(2)}, u32[]{:S(2)}) collective-permute-start(f32[2,128,4]{1,2,0:T(4,128)S(1)} %get-tuple-element.19), channel_id=1, source_target_pairs={{0,1},{1,2},{2,3},{3,4},{4,5},{5,6},{6,7},{7,8},{8,9},{9,10},{10,1... | collective-permute-start | bytes 12296 | tf_op jit(solution)/shard_map/ppermute | solution.py:235
  76.8 1.1 %pad_maximum_fusion.h_ref = f32[2,128,1024]{2,1,0:T(8,128)} fusion(f32[1,128,1024]{2,1,0:T(8,128)S(1)} %fusion.13, f32[1,128,1024]{2,1,0:T(8,128)S(1)} %fusion.12), kind=kLoop, calls=%fused_computation.19 | loop fusion | flops 262144 | bytes 2097152 | tf_op jit(solution)/shard_map/stack | solution.py:220
  77.9 5.6 %collective-permute-done = f32[2,128,4]{1,2,0:T(4,128)S(1)} collective-permute-done((f32[2,128,4]{1,2,0:T(4,128)S(1)}, f32[2,128,4]{1,2,0:T(4,128)S(1)}, u32[]{:S(2)}, u32[]{:S(2)}) %collective-permute-start) | collective-permute-done | bytes 4128 | tf_op jit(solution)/shard_map/ppermute | solution.py:235
  83.5 0.8 copy.31.rim_ref
  84.3 14.7 %shard_map.77 = (f32[6,2,1024]{2,1,0:T(2,128)}, f32[2,1024]{1,0:T(2,128)}) custom-call(f32[2,128,1024]{2,1,0:T(8,128)} %pad_maximum_fusion.h_ref, f32[2,128,8]{2,1,0:T(8,128)} %copy.31.rim_ref, f32[9,1024]{1,0:T(8,128)} %stack.63.w_ref, f32[128,8]{1,0:T(8,128)} %constant.75.clone.phit_ref, f32[32,128]{1,0:T(8,128)} %constant.76.clone.psi_ref), custom_call_target="tpu_custom_call" | custom-call | tf_op jit(solution)/shard_map/pallas_call | solution.py:160
  (19 shorter events, 0.1 us)
Async XLA Ops:
  0.6 1.7 %copy-start.1 = (s32[2048,1]{0,1:T(1,128)S(1)}, s32[2048,1]{0,1:T(1,128)}, u32[]{:S(2)}) copy-start(s32[2048,1]{0,1:T(1,128)} %param.7) | copy-start | bytes 24580
  1.5 1.5 %copy-start.3 = (s32[2048]{0:T(1024)S(1)}, s32[2048]{0:T(1024)}, u32[]{:S(2)}) copy-start(s32[2048]{0:T(1024)} %param.8) | copy-start | bytes 24580
  2.0 1.9 %copy-start = (bf16[2048,3,256]{2,0,1:T(8,128)(2,1)S(1)}, bf16[2048,3,256]{2,0,1:T(8,128)(2,1)}, u32[]{:S(2)}) copy-start(bf16[2048,3,256]{2,0,1:T(8,128)(2,1)} %param.6) | copy-start | bytes 9437188
  19.9 10.5 %copy-start.2 = (s32[4,1024]{1,0:T(4,128)S(1)}, s32[4,1024]{1,0:T(4,128)}, u32[]{:S(2)}) copy-start(s32[4,1024]{1,0:T(4,128)} %param.9) | copy-start | bytes 49156
  20.0 43.0 %all-to-all-start = ((bf16[128,72,128]{2,1,0:T(8,128)(2,1)}), bf16[128,72,128]{2,1,0:T(8,128)(2,1)S(1)}, u32[]{:S(2)}, u32[]{:S(2)}) async-start(bf16[128,72,128]{2,1,0:T(8,128)(2,1)} %fusion.8), calls=%async_computation | async-start | bytes 4718592 | tf_op jit(solution)/shard_map/all_to_all | solution.py:211
  71.0 7.0 %collective-permute-start.1 = (f32[2,128,4]{1,2,0:T(4,128)S(1)}, f32[2,128,4]{1,2,0:T(4,128)S(1)}, u32[]{:S(2)}, u32[]{:S(2)}) collective-permute-start(f32[2,128,4]{1,2,0:T(4,128)S(1)} %get-tuple-element.20), channel_id=1, source_target_pairs={{1,0},{2,1},{3,2},{4,3},{5,4},{6,5},{7,6},{8,7},{9,8},{10,9},{11,1... | collective-permute-start | bytes 12296 | tf_op jit(solution)/shard_map/ppermute | solution.py:236
  74.4 9.1 %collective-permute-start = (f32[2,128,4]{1,2,0:T(4,128)S(1)}, f32[2,128,4]{1,2,0:T(4,128)S(1)}, u32[]{:S(2)}, u32[]{:S(2)}) collective-permute-start(f32[2,128,4]{1,2,0:T(4,128)S(1)} %get-tuple-element.19), channel_id=1, source_target_pairs={{0,1},{1,2},{2,3},{3,4},{4,5},{5,6},{6,7},{7,8},{8,9},{9,10},{10,1... | collective-permute-start | bytes 12296 | tf_op jit(solution)/shard_map/ppermute | solution.py:235
